TPU v7x, 512 devices: a whole 4x8x8 slice. The times are simulated.
512 devices in a mesh: req: 64 (over y, x, core), tp: 8 (over z).
Axes of the slice: x: 4, y: 8, z: 8, core: 2. Of those that a mesh axis runs over, the one named last changes fastest.
Arguments:
- hidden: bfloat16 [2048, 5, 2560], P('req', None, 'tp'), may hold values from -6 to 6
- norm_gain: bfloat16 [2560], replicated, may hold values from 0.099609375 to 1.8984375
- query_weight: bfloat16 [2560, 2560], P(None, 'tp'), may hold values from -0.125 to 0.125
- key_value_matrix: bfloat16 [2560, 8, 160], P(None, 'tp'), may hold values from -0.125 to 0.125
- output_weight: bfloat16 [2560, 2560], P('tp'), may hold values from -0.5 to 0.5
- key_value_cache: bfloat16 [2048, 64, 8, 160], P('req', None, 'tp'), as said below
- deal_order: int32 [2048], P('req'), may hold values from 0 to 2047, as said below
- cache_length: int32 [2048], P('req'), may hold values from 1 to 64, as said below
- accepted: int32 [2048], P('req'), may hold values from 1 to 5
Outputs:
- block_output: bfloat16 [2048, 5, 2560], P('req', None, 'tp')
- new_entries: bfloat16 [2048, 5, 8, 160], P('req', None, 'tp')
Inputs may be any that keep to these rules, and one draw needn't show every extreme that they name: deal_order is a permutation of the 2048 requests; slot i lies on index i // 32 of req, and request r arrives on index r // 32. Every index deals at most 1 of its requests to any one index, and exactly 1 to each of 32 indices. Cache entries of slot i at positions from cache_length[i] on are unused. `key_value_cache`: at positions below cache_length[i] the first 80 entries of each head are the keys, already rotated for their positions, and the last 80 the values.
All inputs are finite; a program needn't handle non-finite values.
Results may differ from a plain program's by a relative error of at most 0.0091.
Values may be sent and summed in bfloat16 or wider, within the bound.
No kernel may reach another device: no remote copies, remote signals or barrier semaphores. Data moves between devices by JAX's collectives and lax.ppermute only.
A program may use at most 128 MiB of HBM per device.

v0:
```python
import math
import jax
import jax.numpy as jnp
from jax import lax
from jax.sharding import PartitionSpec as P

HEAD_SIZE = 80
masked_score = -1e30


def rotate(values, positions):
    half_dim = HEAD_SIZE // 2
    frequency = 10000.0 ** (-2.0 * jnp.arange(half_dim, dtype=jnp.float32) / HEAD_SIZE)
    angles = positions.astype(jnp.float32)[..., None] * frequency
    cosine_part = jnp.cos(angles)
    sine_part = jnp.sin(angles)
    first_half = values[..., :half_dim]
    second_half = values[..., half_dim:]
    return jnp.concatenate(
        [
            first_half * cosine_part - second_half * sine_part,
            second_half * cosine_part + first_half * sine_part,
        ],
        axis=-1,
    )


def attend(query_rows, key_value_cache, fresh, cache_length):
    scale = 1.0 / math.sqrt(HEAD_SIZE)
    slot_count = query_rows.shape[0]
    verified = query_rows.shape[1]
    cache_keys = key_value_cache[..., :HEAD_SIZE]
    cache_values = key_value_cache[..., HEAD_SIZE:]
    fresh_keys = fresh[..., :HEAD_SIZE]
    fresh_values = fresh[..., HEAD_SIZE:]
    cache_scores = (
        jnp.einsum("rtghd,rcgd->rghtc", query_rows, cache_keys, preferred_element_type=jnp.float32)
        * scale
    )
    visible = jnp.arange(key_value_cache.shape[1], dtype=jnp.int32)[None, :] < cache_length[:, None]
    cache_scores = jnp.where(visible[:, None, None, None, :], cache_scores, masked_score)
    fresh_scores = (
        jnp.einsum("rtghd,rugd->rghtu", query_rows, fresh_keys, preferred_element_type=jnp.float32)
        * scale
    )
    causal = (
        jnp.arange(verified, dtype=jnp.int32)[:, None]
        >= jnp.arange(verified, dtype=jnp.int32)[None, :]
    )
    fresh_scores = jnp.where(causal[None, None, None, :, :], fresh_scores, masked_score)
    largest = jnp.maximum(jnp.max(cache_scores, axis=-1), jnp.max(fresh_scores, axis=-1))[..., None]
    cache_expos = jnp.exp(cache_scores - largest)
    fresh_expos = jnp.exp(fresh_scores - largest)
    totals = jnp.sum(cache_expos, axis=-1, keepdims=True) + jnp.sum(
        fresh_expos, axis=-1, keepdims=True
    )
    cache_weights = (cache_expos / totals).astype(jnp.bfloat16)
    fresh_weights = (fresh_expos / totals).astype(jnp.bfloat16)
    mixed = jnp.einsum(
        "rghtc,rcgd->rtghd", cache_weights, cache_values, preferred_element_type=jnp.float32
    )
    mixed = mixed + jnp.einsum(
        "rghtu,rugd->rtghd", fresh_weights, fresh_values, preferred_element_type=jnp.float32
    )
    return mixed.astype(jnp.bfloat16).reshape(slot_count, verified, -1)


def body(
    hidden,
    norm_gain,
    query_weight,
    key_value_matrix,
    output_weight,
    key_value_cache,
    deal_order,
    cache_length,
    accepted,
):
    slot_count = deal_order.shape[0]
    verified = hidden.shape[1]
    device_index = lax.axis_index("req")
    my_requests = device_index * slot_count + jnp.arange(slot_count, dtype=jnp.int32)
    piece = lax.all_gather(hidden, "req", axis=0, tiled=True)
    picker = (deal_order[:, None] == jnp.arange(piece.shape[0], dtype=jnp.int32)[None, :]).astype(
        jnp.bfloat16
    )
    dealt_rows = jnp.einsum(
        "in,ntf->itf", picker, piece, preferred_element_type=jnp.float32
    ).astype(jnp.bfloat16)
    features = lax.all_gather(dealt_rows, "tp", axis=2, tiled=True)
    widened = features.astype(jnp.float32)
    variance = jnp.mean(widened * widened, axis=-1, keepdims=True)
    normed = (widened * lax.rsqrt(variance + 1e-05) * norm_gain.astype(jnp.float32)).astype(
        jnp.bfloat16
    )
    heads_here = query_weight.shape[1] // HEAD_SIZE
    groups_here = key_value_matrix.shape[1]
    positions = cache_length[:, None] + jnp.arange(verified, dtype=jnp.int32)[None, :]
    query_rows = jnp.einsum("rtd,de->rte", normed, query_weight, preferred_element_type=jnp.float32)
    query_rows = query_rows.reshape(
        slot_count, verified, groups_here, heads_here // groups_here, HEAD_SIZE
    )
    query_rows = rotate(query_rows, positions[:, :, None, None]).astype(jnp.bfloat16)
    projected = jnp.einsum(
        "rtd,dge->rtge", normed, key_value_matrix, preferred_element_type=jnp.float32
    )
    fresh = jnp.concatenate(
        [rotate(projected[..., :HEAD_SIZE], positions[:, :, None]), projected[..., HEAD_SIZE:]],
        axis=-1,
    ).astype(jnp.bfloat16)
    keep = (jnp.arange(verified, dtype=jnp.int32)[None, :] < accepted[:, None])[:, :, None, None]
    new_entries = jnp.where(keep, fresh, jnp.zeros_like(fresh))
    mixed = attend(query_rows, key_value_cache, fresh, cache_length)
    partial_sum = jnp.einsum(
        "rte,ed->rtd", mixed, output_weight, preferred_element_type=jnp.float32
    )
    out_dealt = lax.psum_scatter(partial_sum, "tp", scatter_dimension=2, tiled=True).astype(
        jnp.bfloat16
    )
    piece_rows = lax.all_gather(out_dealt, "req", axis=0, tiled=True)
    piece_owners = lax.all_gather(deal_order, "req", axis=0, tiled=True)
    picker = (my_requests[:, None] == piece_owners[None, :]).astype(jnp.bfloat16)
    block_output = jnp.einsum(
        "jn,ntf->jtf", picker, piece_rows, preferred_element_type=jnp.float32
    ).astype(jnp.bfloat16)
    return (block_output, new_entries)


def solution(mesh):
    placed = (
        P("req", None, "tp"),
        P(),
        P(None, "tp"),
        P(None, "tp", None),
        P("tp", None),
        P("req", None, "tp", None),
        P("req"),
        P("req"),
        P("req"),
    )
    return jax.shard_map(
        body,
        mesh=mesh,
        in_specs=placed,
        out_specs=(P("req", None, "tp"), P("req", None, "tp", None)),
        check_vma=False,
    )
```

profile of v0, /device:TPU:1, one launch (start us, length us, event | category | flops | bytes accessed | tf_op | source)
XLA Modules:
  0.0 338.5 jit_solution(15841835390689357700)
XLA Ops:
  7.2 0.0 copy-start
  7.2 0.0 all-gather.3.cloned.1.call-start
  7.2 0.7 all-gather.3.cloned.1.call-update
  7.9 0.0 reduce-scatter.4.cloned.1.call-start
  8.0 0.7 convert_element_type.71
  8.7 0.7 add_convert_fusion
  9.3 0.1 copy.46
  9.4 0.7 iota_compare_fusion.1
  10.2 0.5 multiply_cosine_fusion
  10.7 93.9 %all-gather.3.cloned.1.call-done = bf16[2048,5,320]{2,0,1:T(8,128)(2,1)} async-done(((bf16[32,5,320]{2,0,1:T(8,128)(2,1)}), bf16[2048,5,320]{2,0,1:T(8,128)(2,1)}) %all-gather.3.cloned.1.call-update) | async-done | bytes 6553616 | tf_op jit(solution)/shard_map/all_gather | solution.py:83
  104.6 4.7 %convolution_convert_fusion.1 = bf16[32,5,320]{2,0,1:T(8,128)(2,1)S(1)} fusion(bf16[2048,5,320]{2,0,1:T(8,128)(2,1)} %all-gather.3.cloned.1.call-done, s32[32]{0:T(128)} %param.15), kind=kOutput, calls=%fused_computation.21 | convolution fusion | flops 209831936 | bytes 6656128 | tf_op jit(solution)/shard_map/in,ntf->itf/dot_general | solution.py:87
  109.3 0.4 copy.43
  109.7 55.1 %all_gather.14 = bf16[32,5,2560]{0,1,2:T(8,128)(2,1)} all-gather(bf16[32,5,320]{0,1,2:T(8,128)(2,1)S(1)} %copy.43), channel_id=1, replica_groups=mesh['req'=64,'tp'=8] {'tp'}, dimensions={2}, use_global_device_ids=true | all-gather | bytes 921600 | tf_op jit(solution)/shard_map/all_gather | solution.py:90
  164.9 4.4 %copy.44 = bf16[32,5,2560]{2,0,1:T(8,128)(2,1)S(1)} copy(bf16[32,5,2560]{0,1,2:T(8,128)(2,1)} %all_gather.14) | data formatting | bytes 1638400 | tf_op jit(solution)/shard_map/all_gather | solution.py:90
  169.2 0.0 copy-start.4
  169.3 0.2 fusion
  169.5 1.7 convolution_bitcast_fusion.1
  171.2 0.0 copy-start.1
  171.2 0.1 slice_bitcast_fusion.4
  171.3 0.6 copy-done.1
  171.9 0.4 fusion.41
  172.3 0.0 copy-done.4
  172.3 0.8 fusion.5
  173.1 0.2 reshape.324
  173.3 0.2 fusion.49
  173.5 0.0 copy-start.2
  173.5 0.1 maximum_bitcast_fusion
  173.6 0.5 fusion.24
  174.1 1.4 fusion.51
  175.5 0.0 copy-done.2
  175.5 0.6 fusion.50
  176.1 0.3 fusion.22
  176.3 0.4 fusion.21
  176.8 0.8 convolution_bitcast_fusion
  177.6 0.4 fusion.13
  178.0 0.1 copy.53
  178.1 0.1 reshape.332
  178.2 0.0 copy-done
  178.2 0.6 fusion.3
  178.8 5.5 %copy.64 = f32[32,5,2560]{0,1,2:T(8,128)} copy(f32[32,5,2560]{2,0,1:T(8,128)S(1)} %fusion.3) | data formatting | bytes 3276800
  184.3 8.0 %reshape.347 = f32[2560,160]{1,0:T(8,128)} reshape(f32[2560,5,32]{2,1,0:T(8,128)} %bitcast.87) | data formatting | bytes 3276800
  192.4 0.0 copy-start.3
  192.4 0.0 copy-start.5
  192.4 0.0 reduce-scatter.4.cloned.1.call-update
  192.4 0.0 all-gather.5.cloned.1.call-start
  192.4 39.6 %reduce-scatter.4.cloned.1.call-done = f32[320,160]{1,0:T(8,128)} async-done(((f32[2560,160]{1,0:T(8,128)}), f32[320,160]{1,0:T(8,128)}) %reduce-scatter.4.cloned.1.call-update) | async-done | bytes 204816
  232.1 1.2 reshape.348
  233.3 1.0 copy.65
  234.3 0.0 all-gather.5.cloned.1.call-update
  234.3 1.3 dynamic-slice
  236.3 0.0 copy-done.3
  236.3 0.3 dynamic-update-slice
  236.5 21.3 %all-reduce = s32[2048]{0:T(1024)S(1)} all-reduce(s32[2048]{0:T(1024)S(1)} %dynamic-update-slice), channel_id=1, replica_groups=mesh['req'=64,'tp'=8] {'req'}, use_global_device_ids=true, to_apply=%add | all-reduce | flops 2048 | bytes 16384
  257.9 0.0 copy-done.5
  257.9 1.0 slice.51
  258.9 0.8 fusion.44
  259.7 67.0 %all-gather.5.cloned.1.call-done = bf16[2048,5,320]{2,0,1:T(8,128)(2,1)} async-done(((bf16[32,5,320]{2,0,1:T(8,128)(2,1)}), bf16[2048,5,320]{2,0,1:T(8,128)(2,1)}) %all-gather.5.cloned.1.call-update) | async-done | bytes 6553616 | tf_op jit(solution)/shard_map/all_gather | solution.py:120
  326.7 5.3 %convolution_convert_fusion = bf16[32,5,320]{2,0,1:T(8,128)(2,1)} fusion(bf16[2048,5,320]{2,0,1:T(8,128)(2,1)} %all-gather.5.cloned.1.call-done, s32[2048]{0:T(1024)S(1)} %all-reduce, s32[32]{0:T(128)S(1)} %iota_add_fusion), kind=kOutput, calls=%fused_computation.20 | convolution fusion | flops 209831936 | bytes 6664320 | tf_op jit(solution)/shard_map/jn,ntf->jtf/dot_general | solution.py:123
  (8 shorter events, 0.1 us)
Async XLA Ops:
  7.2 171.1 %copy-start = (bf16[320,2560]{1,0:T(8,128)(2,1)S(1)}, bf16[320,2560]{1,0:T(8,128)(2,1)}, u32[]{:S(2)}) copy-start(bf16[320,2560]{1,0:T(8,128)(2,1)} %param.13) | copy-start | bytes 4915204
  7.2 97.5 %all-gather.3.cloned.1.call-start = ((), (), s32[]{:S(2)}) async-start(), calls=%async_computation.1 | async-start | bytes 7987200 | tf_op jit(solution)/shard_map/all_gather | solution.py:83
  7.9 224.2 %reduce-scatter.4.cloned.1.call-start = ((), (), s32[]{:S(2)}) async-start(), calls=%async_computation.3 | async-start | bytes 2949120
  169.2 3.0 copy-start.4
  171.2 0.7 copy-start.1
  173.5 1.9 copy-start.2
  192.4 43.9 %copy-start.3 = (s32[32]{0:T(128)S(1)}, s32[32]{0:T(128)}, u32[]{:S(2)}) copy-start(s32[32]{0:T(128)} %param.15) | copy-start | bytes 388
  192.4 65.5 %copy-start.5 = (s32[32]{0:T(128)S(1)}, s32[32]{0:T(128)}, u32[]{:S(2)}) copy-start(s32[32]{0:T(128)} %param.17) | copy-start | bytes 388
  192.4 134.3 %all-gather.5.cloned.1.call-start = ((), (), s32[]{:S(2)}) async-start(), calls=%async_computation.2 | async-start | bytes 7987200 | tf_op jit(solution)/shard_map/all_gather | solution.py:120
Sparse Core Ops, SparseCore 0:
  11.3 93.2 all-gather.2
  192.5 39.5 reduce-scatter.3
  235.9 90.6 all-gather.4
where the time goes:
time: 339 us; the launch traced here: 338 us
  waiting for transfers between devices  201 us (59%)
  blocking collectives  76.4 us (23%)
  local copies, waits for them, and re-layouts  24.5 us (7%)
  matrix products  16.2 us (5%)
  between operations  14.6 us (4%)
  other arithmetic  5.35 us (2%)
    all_gather x1, waiting for transfers between devices, body(): piece = lax.all_gather(hidden, 'req', axis=0, tiled=True)  93.9 us
    all_gather x1, waiting for transfers between devices, body(): piece_rows = lax.all_gather(out_dealt, 'req', axis=0, tiled=True)  67 us
    all_gather x1, blocking collectives, body(): features = lax.all_gather(dealt_rows, 'tp', axis=2, tiled=True)  55.1 us
    unnamed x4, waiting for transfers between devices  40.3 us
    unnamed x1, blocking collectives  21.3 us
    unnamed x19, local copies, waits for them, and re-layouts  17.9 us
  transfers between devices with their start and end apart: 3, of which 3 were waited for; matrix products, arithmetic and copies ran while one was open for 2% of the time, Pallas kernels for 0%

commit v1 on v0

--- a/solution.py
+++ b/solution.py
@@ -6,6 +6,12 @@
 
 HEAD_SIZE = 80
 masked_score = -1e30
+
+
+def in_order(pieces, dim):
+    pieces = jnp.moveaxis(pieces, 0, dim)
+    dims = pieces.shape
+    return pieces.reshape(*dims[:dim], dims[dim] * dims[dim + 1], *dims[dim + 2 :])
 
 
 def rotate(values, positions):
@@ -87,7 +93,19 @@
     dealt_rows = jnp.einsum(
         "in,ntf->itf", picker, piece, preferred_element_type=jnp.float32
     ).astype(jnp.bfloat16)
-    features = lax.all_gather(dealt_rows, "tp", axis=2, tiled=True)
+    size = lax.axis_size("tp")
+    pairs = [(i, (i + 1) % size) for i in range(size)]
+    back = [(b, a) for a, b in pairs]
+    lower, upper = ([], [])
+    for hop in range(size - 1):
+        if hop % 2 == 0:
+            lower.append(lax.ppermute(lower[-1] if lower else dealt_rows, "tp", pairs))
+        else:
+            upper.append(lax.ppermute(upper[-1] if upper else dealt_rows, "tp", back))
+    tiles = jnp.stack([*lower[::-1], dealt_rows, *upper])
+    shift = lax.axis_index("tp") - len(lower)
+    tiles = tiles[(jnp.arange(size) - shift) % size]
+    features = in_order(tiles, 2)
     widened = features.astype(jnp.float32)
     variance = jnp.mean(widened * widened, axis=-1, keepdims=True)
     normed = (widened * lax.rsqrt(variance + 1e-05) * norm_gain.astype(jnp.float32)).astype(

time: 339 us -> 323 us (0.953)
  blocking collectives: 76.4 us -> 21 us
  starting transfers between devices: 0.12 us -> 22.8 us
  waiting for transfers between devices: 201 us -> 213 us
  local copies, waits for them, and re-layouts: 24.5 us -> 28.6 us
    all_gather x1 -> x0, blocking collectives: 55.1 us -> none  [body(): features = lax.all_gather(dealt_rows, 'tp', axis=2, tiled=True)]
    ppermute x0 -> x7, starting transfers between devices: none -> 22.7 us  [the longest x3 13.7 us: body(): upper.append(lax.ppermute(upper[-1] if upper else dealt_rows, 'tp', back))]
    ppermute x0 -> x7, waiting for transfers between devices: none -> 6.94 us  [the longest x4 6.93 us: body(): lower.append(lax.ppermute(lower[-1] if lower else dealt_rows, 'tp', pairs))]
    all_gather x1 -> x0, local copies, waits for them, and re-layouts: 4.36 us -> none  [body(): features = lax.all_gather(dealt_rows, 'tp', axis=2, tiled=True)]
    unnamed x19 -> x34, local copies, waits for them, and re-layouts: 17.9 us -> 22.1 us
    unnamed x4, waiting for transfers between devices: 40.3 us -> 44.4 us
  transfers between devices with their start and end apart: 3 -> 10, of which waited for: 3 -> 7; matrix products, arithmetic and copies ran while one was open for 2% -> 3% of each run, Pallas kernels for 0% -> 0%
where the time goes in v1:
time: 323 us
  waiting for transfers between devices  213 us (66%)
  local copies, waits for them, and re-layouts  28.6 us (9%)
  starting transfers between devices  22.8 us (7%)
  blocking collectives  21 us (7%)
  matrix products  17.5 us (5%)
  between operations  14.7 us (5%)
  other arithmetic  4.72 us (1%)
    all_gather x1, waiting for transfers between devices, body(): piece = lax.all_gather(hidden, 'req', axis=0, tiled=True)  95 us
    all_gather x1, waiting for transfers between devices, body(): piece_rows = lax.all_gather(out_dealt, 'req', axis=0, tiled=True)  67 us
    unnamed x4, waiting for transfers between devices  44.4 us
    unnamed x34, local copies, waits for them, and re-layouts  22.1 us
    unnamed x1, blocking collectives  21 us
    ppermute x3, starting transfers between devices, body(): upper.append(lax.ppermute(upper[-1] if upper else dealt_rows, 'tp', back))  13.7 us
    ppermute x4, starting transfers between devices, body(): lower.append(lax.ppermute(lower[-1] if lower else dealt_rows, 'tp', pairs))  9 us
    ppermute x4, waiting for transfers between devices, body(): lower.append(lax.ppermute(lower[-1] if lower else dealt_rows, 'tp', pairs))  6.93 us
  transfers between devices with their start and end apart: 10, of which 7 were waited for; matrix products, arithmetic and copies ran while one was open for 3% of the time, Pallas kernels for 0%

profile of v1, /device:TPU:1, one launch (start us, length us, event | category | flops | bytes accessed | tf_op | source)
XLA Modules:
  0.0 322.7 jit_solution(12114741265236322504)
XLA Ops:
  7.2 0.0 all-gather.3.cloned.1.call-start
  7.2 0.7 all-gather.3.cloned.1.call-update
  7.9 0.0 reduce-scatter.4.cloned.1.call-start
  8.0 0.7 add_convert_fusion.1
  8.6 1.0 multiply_cosine_fusion.1
  9.7 95.0 %all-gather.3.cloned.1.call-done = bf16[2048,5,320]{2,0,1:T(8,128)(2,1)} async-done(((bf16[32,5,320]{2,0,1:T(8,128)(2,1)}), bf16[2048,5,320]{2,0,1:T(8,128)(2,1)}) %all-gather.3.cloned.1.call-update) | async-done | bytes 6553616 | tf_op jit(solution)/shard_map/all_gather | solution.py:89
  104.6 4.7 %convolution_convert_fusion.1 = bf16[32,5,320]{2,0,1:T(8,128)(2,1)S(1)} fusion(bf16[2048,5,320]{2,0,1:T(8,128)(2,1)} %all-gather.3.cloned.1.call-done, s32[32]{0:T(128)} %param.15), kind=kOutput, calls=%fused_computation.21 | convolution fusion | flops 209831936 | bytes 6656128 | tf_op jit(solution)/shard_map/in,ntf->itf/dot_general | solution.py:93
  109.3 3.3 %collective-permute-start = (bf16[32,5,320]{2,0,1:T(8,128)(2,1)S(1)}, bf16[32,5,320]{2,0,1:T(8,128)(2,1)S(1)}, u32[]{:S(2)}, u32[]{:S(2)}) collective-permute-start(bf16[32,5,320]{2,0,1:T(8,128)(2,1)S(1)} %convolution_convert_fusion.1), channel_id=1, source_target_pairs={{0,1},{1,2},{2,3},{3,4},{4,5},{5,6},{6,7},{7,0},{8,9},{9,10},{10,1... | collective-permute-start | bytes 307208 | tf_op jit(solution)/shard_map/ppermute | solution.py:102
  112.6 0.1 iota_compare_fusion.1
  112.7 0.1 reshape.393
  112.8 5.6 %collective-permute-done = bf16[32,5,320]{2,0,1:T(8,128)(2,1)S(1)} collective-permute-done((bf16[32,5,320]{2,0,1:T(8,128)(2,1)S(1)}, bf16[32,5,320]{2,0,1:T(8,128)(2,1)S(1)}, u32[]{:S(2)}, u32[]{:S(2)}) %collective-permute-start) | collective-permute-done | bytes 102432 | tf_op jit(solution)/shard_map/ppermute | solution.py:102
  118.4 1.9 collective-permute-start.1
  120.3 4.6 %collective-permute-start.4 = (bf16[32,5,320]{2,0,1:T(8,128)(2,1)S(1)}, bf16[32,5,320]{2,0,1:T(8,128)(2,1)S(1)}, u32[]{:S(2)}, u32[]{:S(2)}) collective-permute-start(bf16[32,5,320]{2,0,1:T(8,128)(2,1)S(1)} %convolution_convert_fusion.1), channel_id=1, source_target_pairs={{1,0},{2,1},{3,2},{4,3},{5,4},{6,5},{7,6},{0,7},{9,8},{10,9},{11,1... | collective-permute-start | bytes 307208 | tf_op jit(solution)/shard_map/ppermute | solution.py:104
  124.9 0.7 collective-permute-done.1
  125.6 1.9 collective-permute-start.2
  127.5 4.6 %collective-permute-start.5 = (bf16[32,5,320]{2,0,1:T(8,128)(2,1)S(1)}, bf16[32,5,320]{2,0,1:T(8,128)(2,1)S(1)}, u32[]{:S(2)}, u32[]{:S(2)}) collective-permute-start(bf16[32,5,320]{2,0,1:T(8,128)(2,1)S(1)} %collective-permute-done.4), channel_id=1, source_target_pairs={{1,0},{2,1},{3,2},{4,3},{5,4},{6,5},{7,6},{0,7},{9,8},{10,9},{11,1... | collective-permute-start | bytes 307208 | tf_op jit(solution)/shard_map/ppermute | solution.py:104
  132.1 0.3 collective-permute-done.2
  132.4 1.9 collective-permute-start.3
  134.4 4.6 %collective-permute-start.6 = (bf16[32,5,320]{2,0,1:T(8,128)(2,1)S(1)}, bf16[32,5,320]{2,0,1:T(8,128)(2,1)S(1)}, u32[]{:S(2)}, u32[]{:S(2)}) collective-permute-start(bf16[32,5,320]{2,0,1:T(8,128)(2,1)S(1)} %collective-permute-done.5), channel_id=1, source_target_pairs={{1,0},{2,1},{3,2},{4,3},{5,4},{6,5},{7,6},{0,7},{9,8},{10,9},{11,1... | collective-permute-start | bytes 307208 | tf_op jit(solution)/shard_map/ppermute | solution.py:104
  139.0 0.3 collective-permute-done.3
  139.3 0.7 bitcast_dynamic-update-slice_fusion.7
  139.9 0.7 bitcast_dynamic-update-slice_fusion.6
  140.6 0.6 bitcast_dynamic-update-slice_fusion.5
  141.2 0.7 bitcast_dynamic-update-slice_fusion.4
  141.9 0.7 bitcast_dynamic-update-slice_fusion.3
  142.5 0.7 bitcast_dynamic-update-slice_fusion.2
  143.2 0.7 bitcast_dynamic-update-slice_fusion.1
  143.9 0.7 bitcast_dynamic-update-slice_fusion
  144.6 2.0 gather_fusion
  146.5 0.3 fusion
  146.8 0.3 fusion.12
  147.2 0.3 copy.29
  147.5 0.7 convert_element_type.82
  148.2 1.6 reshape.408
  149.7 1.6 convolution_bitcast_fusion.2
  151.3 0.4 fusion.37
  151.7 0.1 slice_bitcast_fusion.4
  151.8 0.1 maximum_bitcast_fusion
  151.9 0.1 copy-done.1
  152.0 0.9 convolution_bitcast_fusion.1
  152.9 0.2 fusion.27
  153.1 0.1 pad_maximum_fusion
  153.2 1.3 fusion.46
  154.6 0.5 fusion.45
  155.1 0.3 fusion.16
  155.4 0.4 fusion.15
  155.9 0.9 convolution_bitcast_fusion
  156.7 0.4 fusion.11
  157.1 0.1 copy.37
  157.2 0.1 reshape.392
  157.3 2.0 fusion.3
  159.3 5.5 %copy.49 = f32[32,5,2560]{0,1,2:T(8,128)} copy(f32[32,5,2560]{2,0,1:T(8,128)S(1)} %fusion.3) | data formatting | bytes 3276800
  164.8 8.0 %reshape.418 = f32[2560,160]{1,0:T(8,128)} reshape(f32[2560,5,32]{2,1,0:T(8,128)} %bitcast.123) | data formatting | bytes 3276800
  172.9 0.0 all-gather.5.cloned.1.call-start
  172.9 43.7 %reduce-scatter.4.cloned.1.call-done = f32[320,160]{1,0:T(8,128)} async-done(((f32[2560,160]{1,0:T(8,128)}), f32[320,160]{1,0:T(8,128)}) %reduce-scatter.4.cloned.1.call-update) | async-done | bytes 204816
  216.6 1.2 reshape.419
  217.8 1.0 copy.50
  218.8 1.3 dynamic-slice
  220.8 0.3 dynamic-update-slice
  221.1 21.0 %all-reduce = s32[2048]{0:T(1024)S(1)} all-reduce(s32[2048]{0:T(1024)S(1)} %dynamic-update-slice), channel_id=1, replica_groups=mesh['req'=64,'tp'=8] {'req'}, use_global_device_ids=true, to_apply=%add | all-reduce | flops 2048 | bytes 16384
  242.1 1.0 slice.65
  243.1 0.8 fusion.40
  243.9 67.0 %all-gather.5.cloned.1.call-done = bf16[2048,5,320]{2,0,1:T(8,128)(2,1)} async-done(((bf16[32,5,320]{2,0,1:T(8,128)(2,1)}), bf16[2048,5,320]{2,0,1:T(8,128)(2,1)}) %all-gather.5.cloned.1.call-update) | async-done | bytes 6553616 | tf_op jit(solution)/shard_map/all_gather | solution.py:138
  310.9 5.3 %convolution_convert_fusion = bf16[32,5,320]{2,0,1:T(8,128)(2,1)} fusion(bf16[2048,5,320]{2,0,1:T(8,128)(2,1)} %all-gather.5.cloned.1.call-done, s32[2048]{0:T(1024)S(1)} %all-reduce, s32[32]{0:T(128)S(1)} %iota_add_fusion), kind=kOutput, calls=%fused_computation.20 | convolution fusion | flops 209831936 | bytes 6664320 | tf_op jit(solution)/shard_map/jn,ntf->jtf/dot_general | solution.py:141
  (34 shorter events, 0.2 us)
Async XLA Ops:
  7.2 144.8 %copy-start = (bf16[2560,320]{0,1:T(8,128)(2,1)S(1)}, bf16[2560,320]{0,1:T(8,128)(2,1)}, u32[]{:S(2)}) copy-start(bf16[2560,320]{0,1:T(8,128)(2,1)} %param.11) | copy-start | bytes 4915204
  7.2 97.5 %all-gather.3.cloned.1.call-start = ((), (), s32[]{:S(2)}) async-start(), calls=%async_computation.1 | async-start | bytes 7987200 | tf_op jit(solution)/shard_map/all_gather | solution.py:89
  7.9 208.7 %reduce-scatter.4.cloned.1.call-start = ((), (), s32[]{:S(2)}) async-start(), calls=%async_computation.3 | async-start | bytes 2949120
  9.7 102.9 %copy-start.7 = (s32[32]{0:T(128)S(1)}, s32[32]{0:T(128)}, u32[]{:S(2)}) copy-start(s32[32]{0:T(128)} %param.16) | copy-start | bytes 388
  9.7 103.0 %copy-start.6 = (bf16[2560]{0:T(1024)(128)(2,1)S(1)}, bf16[2560]{0:T(1024)(128)(2,1)}, u32[]{:S(2)}) copy-start(bf16[2560]{0:T(1024)(128)(2,1)} %param.10) | copy-start | bytes 15364
  109.3 9.1 %collective-permute-start = (bf16[32,5,320]{2,0,1:T(8,128)(2,1)S(1)}, bf16[32,5,320]{2,0,1:T(8,128)(2,1)S(1)}, u32[]{:S(2)}, u32[]{:S(2)}) collective-permute-start(bf16[32,5,320]{2,0,1:T(8,128)(2,1)S(1)} %convolution_convert_fusion.1), channel_id=1, source_target_pairs={{0,1},{1,2},{2,3},{3,4},{4,5},{5,6},{6,7},{7,0},{8,9},{9,10},{10,1... | collective-permute-start | bytes 307208 | tf_op jit(solution)/shard_map/ppermute | solution.py:102
  118.4 7.2 %collective-permute-start.1 = (bf16[32,5,320]{2,0,1:T(8,128)(2,1)S(1)}, bf16[32,5,320]{2,0,1:T(8,128)(2,1)S(1)}, u32[]{:S(2)}, u32[]{:S(2)}) collective-permute-start(bf16[32,5,320]{2,0,1:T(8,128)(2,1)S(1)} %collective-permute-done), channel_id=1, source_target_pairs={{0,1},{1,2},{2,3},{3,4},{4,5},{5,6},{6,7},{7,0},{8,9},{9,10},{10,1... | collective-permute-start | bytes 307208 | tf_op jit(solution)/shard_map/ppermute | solution.py:102
  120.3 7.2 %collective-permute-start.4 = (bf16[32,5,320]{2,0,1:T(8,128)(2,1)S(1)}, bf16[32,5,320]{2,0,1:T(8,128)(2,1)S(1)}, u32[]{:S(2)}, u32[]{:S(2)}) collective-permute-start(bf16[32,5,320]{2,0,1:T(8,128)(2,1)S(1)} %convolution_convert_fusion.1), channel_id=1, source_target_pairs={{1,0},{2,1},{3,2},{4,3},{5,4},{6,5},{7,6},{0,7},{9,8},{10,9},{11,1... | collective-permute-start | bytes 307208 | tf_op jit(solution)/shard_map/ppermute | solution.py:104
  125.6 6.8 %collective-permute-start.2 = (bf16[32,5,320]{2,0,1:T(8,128)(2,1)S(1)}, bf16[32,5,320]{2,0,1:T(8,128)(2,1)S(1)}, u32[]{:S(2)}, u32[]{:S(2)}) collective-permute-start(bf16[32,5,320]{2,0,1:T(8,128)(2,1)S(1)} %collective-permute-done.1), channel_id=1, source_target_pairs={{0,1},{1,2},{2,3},{3,4},{4,5},{5,6},{6,7},{7,0},{8,9},{9,10},{10,1... | collective-permute-start | bytes 307208 | tf_op jit(solution)/shard_map/ppermute | solution.py:102
  127.5 6.8 %collective-permute-start.5 = (bf16[32,5,320]{2,0,1:T(8,128)(2,1)S(1)}, bf16[32,5,320]{2,0,1:T(8,128)(2,1)S(1)}, u32[]{:S(2)}, u32[]{:S(2)}) collective-permute-start(bf16[32,5,320]{2,0,1:T(8,128)(2,1)S(1)} %collective-permute-done.4), channel_id=1, source_target_pairs={{1,0},{2,1},{3,2},{4,3},{5,4},{6,5},{7,6},{0,7},{9,8},{10,9},{11,1... | collective-permute-start | bytes 307208 | tf_op jit(solution)/shard_map/ppermute | solution.py:104
  132.4 6.8 %collective-permute-start.3 = (bf16[32,5,320]{2,0,1:T(8,128)(2,1)S(1)}, bf16[32,5,320]{2,0,1:T(8,128)(2,1)S(1)}, u32[]{:S(2)}, u32[]{:S(2)}) collective-permute-start(bf16[32,5,320]{2,0,1:T(8,128)(2,1)S(1)} %collective-permute-done.2), channel_id=1, source_target_pairs={{0,1},{1,2},{2,3},{3,4},{4,5},{5,6},{6,7},{7,0},{8,9},{9,10},{10,1... | collective-permute-start | bytes 307208 | tf_op jit(solution)/shard_map/ppermute | solution.py:102
  134.4 9.5 %collective-permute-start.6 = (bf16[32,5,320]{2,0,1:T(8,128)(2,1)S(1)}, bf16[32,5,320]{2,0,1:T(8,128)(2,1)S(1)}, u32[]{:S(2)}, u32[]{:S(2)}) collective-permute-start(bf16[32,5,320]{2,0,1:T(8,128)(2,1)S(1)} %collective-permute-done.5), channel_id=1, source_target_pairs={{1,0},{2,1},{3,2},{4,3},{5,4},{6,5},{7,6},{0,7},{9,8},{10,9},{11,1... | collective-permute-start | bytes 307208 | tf_op jit(solution)/shard_map/ppermute | solution.py:104
  149.7 2.3 copy-start.2
  151.3 0.7 copy-start.1
  152.0 0.9 copy-start.3
  152.0 0.9 copy-start.4
  152.9 1.7 copy-start.5
  172.8 47.9 %copy-start.8 = (s32[32]{0:T(128)S(1)}, s32[32]{0:T(128)}, u32[]{:S(2)}) copy-start(s32[32]{0:T(128)} %param.15) | copy-start | bytes 388
  172.8 69.2 %copy-start.9 = (s32[32]{0:T(128)S(1)}, s32[32]{0:T(128)}, u32[]{:S(2)}) copy-start(s32[32]{0:T(128)} %param.17) | copy-start | bytes 388
  172.9 138.0 %all-gather.5.cloned.1.call-start = ((), (), s32[]{:S(2)}) async-start(), calls=%async_computation.2 | async-start | bytes 7987200 | tf_op jit(solution)/shard_map/all_gather | solution.py:138
Sparse Core Ops, SparseCore 0:
  11.3 93.2 all-gather.2
  173.0 43.5 reduce-scatter.3
  220.4 90.3 all-gather.4
